TPU v7x, 128 devices: a whole 4x4x4 slice. The times are simulated.
128 devices in a mesh: row: 8 (over y, core), col: 16 (over x, z).
Axes of the slice: x: 4, y: 4, z: 4, core: 2. Of those that a mesh axis runs over, the one named last changes fastest.
Arguments:
- tokens: bfloat16 [10240, 3200], P('col', 'row'), may hold values from -24 to 24
- w_qkv: bfloat16 [3200, 9600], P('row', 'col'), may hold values from -4 to 4
- q_gain: float32 [3200], replicated, may hold values from 0.5 to 1.5
- k_gain: float32 [3200], replicated, may hold values from 0.5 to 1.5
- segment_ids: int32 [8, 1280], P('row'), may hold values from 0 to 3, never falling along the last dimension, each value on 1 to 640 neighbouring positions
Outputs:
- attended: bfloat16 [10240, 3200], P(('row', 'col'))
Inputs may be any that keep to these rules, and one draw needn't show every extreme that they name: `segment_ids`: in each pack the ids never fall; each of the 4 images holds 1 to 640 tokens, one exactly 640.
All inputs are finite; a program needn't handle non-finite values.
Results may differ from a plain program's by a relative error of at most 0.033.
Values may be sent and summed in bfloat16 or wider, within the bound.
No kernel may reach another device: no remote copies, remote signals or barrier semaphores. Data moves between devices by JAX's collectives and lax.ppermute only.
A program may use at most 192 MiB of HBM per device.

v0:
```python
import jax
import jax.numpy as jnp
from jax import lax
from jax.sharding import PartitionSpec as P

ATTENTION_HEADS = 25
HEAD_WIDTH = 128
TOK_DEV = 80


def rms_norm(block, gain):
    values = block.astype(jnp.float32)
    mean_sq = jnp.mean(values * values, axis=-1, keepdims=True)
    return (values * lax.rsqrt(mean_sq + 1e-06) * gain).astype(jnp.bfloat16)


def attend(carry, queries, query_ids, keys, values, key_ids):
    best, total, accum = carry
    count_q = queries.shape[0]
    count_k = keys.shape[0]
    q3 = queries.reshape(count_q, ATTENTION_HEADS, HEAD_WIDTH)
    k3 = keys.reshape(count_k, ATTENTION_HEADS, HEAD_WIDTH)
    value_three = values.reshape(count_k, ATTENTION_HEADS, HEAD_WIDTH)
    scores = jnp.einsum(
        "qhd,khd->hqk", q3, k3, preferred_element_type=jnp.float32
    ) * HEAD_WIDTH ** (-0.5)
    mask = (query_ids[:, None] == key_ids[None, :])[None]
    masked = jnp.where(mask, scores, -1e30)
    new_best = jnp.maximum(best, jnp.max(masked, axis=-1))
    expo = jnp.where(mask, jnp.exp(masked - new_best[..., None]), 0.0)
    ratio = jnp.exp(best - new_best)
    total = total * ratio + jnp.sum(expo, axis=-1)
    weights = expo.astype(jnp.bfloat16)
    update = jnp.einsum("hqk,khd->hqd", weights, value_three, preferred_element_type=jnp.float32)
    return (new_best, total, accum * ratio[..., None] + update)


def local(tokens, w_qkv, q_gain, k_gain, segment_ids):
    width = q_gain.shape[0]
    tok_count = TOK_DEV
    position = lax.axis_index("col")
    partial_sums = jnp.dot(
        lax.all_gather(tokens, "col", axis=0, tiled=True), w_qkv, preferred_element_type=jnp.float32
    )
    summed = lax.psum_scatter(
        partial_sums.astype(jnp.bfloat16), "row", scatter_dimension=0, tiled=True
    )
    pack_ids = segment_ids[0]
    query_ids = lax.dynamic_slice_in_dim(pack_ids, position * tok_count, tok_count, 0)
    start_carry = (
        jnp.full((ATTENTION_HEADS, tok_count), -1e30, jnp.float32),
        jnp.zeros((ATTENTION_HEADS, tok_count), jnp.float32),
        jnp.zeros((ATTENTION_HEADS, tok_count, HEAD_WIDTH), jnp.float32),
    )
    whole = lax.all_gather(summed, "col", axis=1, tiled=True)
    own_rows = lax.dynamic_slice_in_dim(whole, position * tok_count, tok_count, 0)
    normed_q = rms_norm(own_rows[:, :width], q_gain)
    normed_k = rms_norm(whole[:, width : 2 * width], k_gain)
    all_values = whole[:, 2 * width :]
    block_rows = whole.shape[0] // 4
    carry = start_carry
    for block in range(4):
        lower = block * block_rows
        keys = normed_k[lower : lower + block_rows]
        key_ids = lax.dynamic_slice_in_dim(pack_ids, lower, keys.shape[0], 0)
        carry = attend(
            carry, normed_q, query_ids, keys, all_values[lower : lower + block_rows], key_ids
        )
    best, total, accum = carry
    result = accum / total[..., None]
    return jnp.transpose(result, (1, 0, 2)).reshape(tok_count, width).astype(jnp.bfloat16)


def solution(mesh):
    return jax.shard_map(
        local,
        mesh=mesh,
        in_specs=(P("col", "row"), P("row", "col"), P(), P(), P("row", None)),
        out_specs=P(("row", "col"), None),
        check_vma=False,
    )
```

profile of v0, /device:TPU:8, one launch (start us, length us, event | category | flops | bytes accessed | tf_op | source)
XLA Modules:
  0.0 367.9 jit_solution(6712530993973618767)
XLA Ops:
  6.5 0.0 copy-start
  6.5 0.0 all-gather.3.cloned.1.call-start
  6.5 0.7 all-gather.3.cloned.1.call-update
  7.3 0.0 reduce-scatter.2.cloned.1.call-start
  7.3 74.5 %all-gather.3.cloned.1.call-done = bf16[10240,400]{0,1:T(8,128)(2,1)} async-done(((bf16[640,400]{0,1:T(8,128)(2,1)}), bf16[10240,400]{0,1:T(8,128)(2,1)}) %all-gather.3.cloned.1.call-update) | async-done | bytes 8192016 | tf_op jit(solution)/shard_map/all_gather | solution.py:43
  81.8 0.0 copy-done
  81.8 11.5 %convolution_convert_fusion = bf16[10240,600]{0,1:T(8,128)(2,1)} fusion(bf16[10240,400]{0,1:T(8,128)(2,1)} %all-gather.3.cloned.1.call-done, bf16[400,600]{1,0:T(8,128)(2,1)S(1)} %copy-done), kind=kOutput, calls=%fused_computation.5 | convolution fusion | flops 4921344000 | bytes 20960000 | tf_op jit(solution)/shard_map/dot_general | solution.py:42
  93.3 0.0 copy-start.4
  93.3 0.0 reduce-scatter.2.cloned.1.call-update
  93.3 0.0 all-gather.5.cloned.1.call-start
  93.4 68.4 %reduce-scatter.2.cloned.1.call-done = bf16[1280,600]{0,1:T(8,128)(2,1)} async-done(((bf16[10240,600]{0,1:T(8,128)(2,1)}), bf16[1280,600]{0,1:T(8,128)(2,1)}) %reduce-scatter.2.cloned.1.call-update) | async-done | bytes 1536016 | tf_op jit(solution)/shard_map/reduce_scatter | solution.py:45
  161.8 0.0 all-gather.5.cloned.1.call-update
  161.8 0.0 copy-done.4
  161.8 0.1 dynamic-slice_bitcast_fusion
  161.9 0.1 slice_reduce_fusion
  162.0 0.1 broadcast_compare_fusion.1
  162.2 155.1 %all-gather.5.cloned.1.call-done = bf16[1280,9600]{0,1:T(8,128)(2,1)} async-done(((bf16[1280,600]{0,1:T(8,128)(2,1)}), bf16[1280,9600]{0,1:T(8,128)(2,1)}) %all-gather.5.cloned.1.call-update) | async-done | bytes 24576016 | tf_op jit(solution)/shard_map/all_gather | solution.py:55
  317.3 1.9 fusion.15
  319.2 0.0 copy-start.3
  319.2 5.0 %fusion = f32[1280]{0:T(1024)S(1)} fusion(bf16[1280,9600]{0,1:T(8,128)(2,1)} %all-gather.5.cloned.1.call-done), kind=kLoop, calls=%fused_computation.2 | loop fusion | flops 12286720 | bytes 8197120 | tf_op jit(solution)/shard_map/reduce_sum | solution.py:13
  324.3 0.0 copy-done.3
  324.3 5.4 %fusion.2 = bf16[1280,3200]{0,1:T(8,128)(2,1)S(1)} fusion(f32[3200]{0:T(1024)S(1)} %copy-done.3, f32[1280]{0:T(1024)S(1)} %add_rsqrt_fusion, bf16[1280,9600]{0,1:T(8,128)(2,1)} %all-gather.5.cloned.1.call-done), kind=kLoop, calls=%fused_computation.4 | loop fusion | flops 16384000 | bytes 16401920 | tf_op jit(solution)/shard_map/convert_element_type | solution.py:14
  329.6 0.0 copy-start.2
  329.7 3.3 fusion.108
  332.9 0.0 copy-done.2
  332.9 2.1 fusion.17
  335.1 0.9 fusion.6
  336.0 0.9 fusion.5
  336.9 0.9 fusion.4
  337.8 0.9 fusion.3
  338.8 2.5 fusion.11
  341.3 2.5 fusion.7
  343.9 5.7 %fusion.107 = (bf16[320,3200]{0,1:T(8,128)(2,1)S(1)}, bf16[320,3200]{0,1:T(8,128)(2,1)S(1)}, bf16[320,3200]{0,1:T(8,128)(2,1)S(1)}, bf16[320,3200]{0,1:T(8,128)(2,1)S(1)}) fusion(bf16[1280,9600]{0,1:T(8,128)(2,1)} %all-gather.5.cloned.1.call-done), kind=kLoop, calls=%fused_computation.112 | loop fusion | bytes 16384000 | tf_op jit(solution)/shard_map/slice | solution.py:67
  349.5 2.7 fusion.76
  352.2 2.9 fusion.70
  355.1 2.7 fusion.64
  357.8 0.0 copy-start.1
  357.8 2.7 fusion.81
  360.5 0.9 copy.45
  361.3 0.0 copy-done.1
  (4 shorter events, 0.1 us)
Async XLA Ops:
  6.5 75.3 %copy-start = (bf16[400,600]{1,0:T(8,128)(2,1)S(1)}, bf16[400,600]{1,0:T(8,128)(2,1)}, u32[]{:S(2)}) copy-start(bf16[400,600]{1,0:T(8,128)(2,1)} %param.6) | copy-start | bytes 1440004
  6.5 75.3 %all-gather.3.cloned.1.call-start = ((), (), s32[]{:S(2)}) async-start(), calls=%async_computation.1 | async-start | bytes 8704000 | tf_op jit(solution)/shard_map/all_gather | solution.py:43
  7.3 154.5 %reduce-scatter.2.cloned.1.call-start = ((), (), s32[]{:S(2)}) async-start(), calls=%async_computation.2 | async-start | bytes 13824000 | tf_op jit(solution)/shard_map/reduce_scatter | solution.py:45
  93.3 68.5 %copy-start.4 = (s32[1,1280]{1,0:T(1,128)S(1)}, s32[1,1280]{1,0:T(1,128)}, u32[]{:S(2)}) copy-start(s32[1,1280]{1,0:T(1,128)} %param.9) | copy-start | bytes 15364
  93.3 223.9 %all-gather.5.cloned.1.call-start = ((), (), s32[]{:S(2)}) async-start(), calls=%async_computation.3 | async-start | bytes 26112000 | tf_op jit(solution)/shard_map/all_gather | solution.py:55
  319.2 5.0 %copy-start.3 = (f32[3200]{0:T(1024)S(1)}, f32[3200]{0:T(1024)}, u32[]{:S(2)}) copy-start(f32[3200]{0:T(1024)} %param.8) | copy-start | bytes 38404
  329.6 3.3 copy-start.2
  357.8 3.6 copy-start.1
Sparse Core Ops, SparseCore 0:
  9.5 72.2 all-gather.2
  93.5 68.2 reduce-scatter.1
  164.0 153.2 all-gather.4
where the time goes:
time: 369 us; the launch traced here: 368 us
  waiting for transfers between devices  299 us (81%)
  matrix products  26.1 us (7%)
  other arithmetic  19.7 us (5%)
  between operations  13.3 us (4%)
  local copies, waits for them, and re-layouts  9.99 us (3%)
    all_gather x1, waiting for transfers between devices, local(): whole = lax.all_gather(summed, 'col', axis=1, tiled=True)  155 us
    all_gather x1, waiting for transfers between devices, local(): lax.all_gather(tokens, 'col', axis=0, tiled=True)  74.5 us
    reduce_scatter x1, waiting for transfers between devices, local(): lax.psum_scatter(partial_sums.astype(jnp.bfloat16), 'row', scatter_dimens...  68.4 us
    dot_general x1, matrix products, local(): jnp.dot(lax.all_gather(tokens, 'col', axis=0, tiled=True), w_qkv, preferr...  11.5 us
    dot_general x4, matrix products, attend(): jnp.einsum('hqk,khd->hqd', weights, value_three, preferred_element_type=j...  10.9 us
    convert_element_type x2, other arithmetic, rms_norm(): return (values * lax.rsqrt(mean_sq + 1e-06) * gain).astype(jnp.bfloat16)  7.52 us
  transfers between devices with their start and end apart: 3, of which 3 were waited for; matrix products, arithmetic and copies ran while one was open for 0% of the time, Pallas kernels for 0%

commit v1 on v0

v1 whole, which is shorter than its diff:
```python
import numpy as np
import jax
import jax.numpy as jnp
from jax import lax
from jax.sharding import Mesh, PartitionSpec as P

ATTENTION_HEADS = 25
HEAD_WIDTH = 128
ROW = ("y", "k")
COL = ("x", "z")


def build_local(nx, nz):
    nc = nx * nz

    def col_of_rho(rho):
        return (rho % nx) * nz + rho // nx

    perms, regions = [], np.zeros((nc, 3), np.int32)
    for j in range(3):
        pairs = []
        for src in range(nc):
            rho = (3 * src + j) % nc
            regions[rho, j] = (3 * src + j) // nc
            pairs.append((src, col_of_rho(rho)))
        perms.append(pairs)
    assert all(sorted(regions[r]) == [0, 1, 2] for r in range(nc))

    def head_table(width):
        piece = width // nc
        h0 = np.zeros(nc, np.int32)
        off = np.zeros((nc, 2), np.int32)
        owner = []
        for rho in range(nc):
            lo, hi = piece * rho, piece * (rho + 1)
            hs = [h for h in range(ATTENTION_HEADS) if lo <= h * HEAD_WIDTH < hi]
            assert 1 <= len(hs) <= 2
            for slot in range(2):
                o = (hs[0] + slot) * HEAD_WIDTH - lo
                off[rho, slot] = min(o, piece)
            for slot, h in enumerate(hs):
                owner.append((h, col_of_rho(rho), slot))
        owner.sort()
        assert [o[0] for o in owner] == list(range(ATTENTION_HEADS))
        gather = np.array([c * 2 + s for _, c, s in owner], np.int32)
        return off, gather

    shift_pairs = [(col_of_rho(r + 1), col_of_rho(r)) for r in range(nc - 1)]

    def local(tokens, w_qkv, q_gain, k_gain, segment_ids):
        tok_blk, feat_blk = tokens.shape
        width = q_gain.shape[0]
        piece = width // nc
        quarter = tok_blk // nx
        pack_tokens = segment_ids.shape[1]
        x = lax.axis_index("x")
        z = lax.axis_index("z")
        rho = z * nx + x
        off_tab, gather_idx = head_table(width)

        wp = w_qkv.reshape(feat_blk, 3, piece)
        got = [lax.ppermute(wp[:, j, :], COL, perms[j]) for j in range(3)]
        reg = jnp.asarray(regions)[rho]
        wr = []
        for s in range(3):
            acc = jnp.where(reg[0] == s, got[0], got[1])
            acc = jnp.where(reg[2] == s, got[2], acc)
            wr.append(acc)
        wr = jnp.stack(wr, axis=1)
        wg = lax.all_gather(wr, "x", axis=2, tiled=False)
        wg = wg.reshape(feat_blk, 3 * nx * piece)

        tq = tokens.reshape(nx, quarter, feat_blk)
        tq = lax.all_to_all(tq, "x", 0, 0, tiled=True)
        tq = lax.all_gather(tq, "z", axis=0, tiled=False)
        tq = jnp.transpose(tq, (1, 0, 2, 3)).reshape(nc * quarter, feat_blk)

        part = jnp.dot(tq, wg, preferred_element_type=jnp.float32).astype(jnp.bfloat16)
        n_packs = nc // 2
        part = part.reshape(n_packs, 2 * quarter, 3 * nx * piece)
        mine = lax.psum_scatter(part, ROW, scatter_dimension=0, tiled=True)[0]
        mine = mine.reshape(2 * quarter, 3, nx * piece)

        qv = mine[:, 0, :].astype(jnp.float32)
        kv = mine[:, 1, :].astype(jnp.float32)
        sums = jnp.stack([jnp.sum(qv * qv, axis=-1), jnp.sum(kv * kv, axis=-1)], axis=-1)
        sums = lax.psum(sums, "z")
        rs = lax.rsqrt(sums / width + 1e-06)
        qg = lax.dynamic_slice_in_dim(q_gain, z * nx * piece, nx * piece)
        kg = lax.dynamic_slice_in_dim(k_gain, z * nx * piece, nx * piece)
        nq = (qv * rs[:, 0:1] * qg).astype(jnp.bfloat16)
        nk = (kv * rs[:, 1:2] * kg).astype(jnp.bfloat16)
        normed = jnp.stack([nq, nk, mine[:, 2, :]], axis=1)

        normed = normed.reshape(2 * quarter, 3, nx, piece)
        sl = lax.all_to_all(normed, "x", 2, 0, tiled=True)
        sl = sl.reshape(pack_tokens, 3, piece)
        ext = lax.ppermute(sl[:, :, :HEAD_WIDTH], COL, shift_pairs)
        sl = jnp.concatenate([sl, ext], axis=2)

        offs = jnp.asarray(off_tab)[rho]
        heads = jnp.stack(
            [lax.dynamic_slice_in_dim(sl, offs[i], HEAD_WIDTH, axis=2) for i in range(2)], axis=2
        )
        q3 = heads[:, 0]
        k3 = heads[:, 1]
        v3 = heads[:, 2]

        ids = segment_ids[0].reshape(2, nx, quarter).transpose(1, 0, 2).reshape(pack_tokens)
        scores = jnp.einsum("qhd,khd->hqk", q3, k3, preferred_element_type=jnp.float32)
        scores = scores * HEAD_WIDTH ** (-0.5)
        mask = (ids[:, None] == ids[None, :])[None]
        masked = jnp.where(mask, scores, -1e30)
        top = jnp.max(masked, axis=-1, keepdims=True)
        expo = jnp.where(mask, jnp.exp(masked - top), 0.0)
        total = jnp.sum(expo, axis=-1)
        weights = expo.astype(jnp.bfloat16)
        summed = jnp.einsum("hqk,khd->hqd", weights, v3, preferred_element_type=jnp.float32)
        res = (summed / total[..., None]).astype(jnp.bfloat16)

        tpc = pack_tokens // nc
        res = res.reshape(2, nx, 2, quarter // tpc, tpc, HEAD_WIDTH)
        res = jnp.transpose(res, (2, 1, 3, 4, 0, 5)).reshape(nc, tpc, 2, HEAD_WIDTH)
        back = lax.all_to_all(res, COL, 0, 0, tiled=True)
        back = jnp.transpose(back, (0, 2, 1, 3)).reshape(nc * 2, tpc, HEAD_WIDTH)
        out = jnp.take(back, jnp.asarray(gather_idx), axis=0)
        return jnp.transpose(out, (1, 0, 2)).reshape(tpc, width)

    return local


def solution(mesh):
    nr, nc = mesh.devices.shape
    nx = 4
    nz = nc // nx
    m4 = Mesh(mesh.devices.reshape(nr // 2, 2, nx, nz), ("y", "k", "x", "z"))
    return jax.shard_map(
        build_local(nx, nz),
        mesh=m4,
        in_specs=(P(COL, ROW), P(ROW, COL), P(), P(), P(ROW, None)),
        out_specs=P(ROW + COL, None),
        check_vma=False,
    )
```

time: 369 us -> 316 us (0.86)
  waiting for transfers between devices: 299 us -> 174 us
  local copies, waits for them, and re-layouts: 9.99 us -> 38.1 us
  blocking collectives: 0 us -> 26 us
  starting transfers between devices: 0.08 us -> 23.1 us
  other arithmetic: 19.7 us -> 5.5 us
  between operations: 13.3 us -> 21.3 us
    all_gather x2, waiting for transfers between devices: 230 us -> 56.5 us  [the longest x1 34.2 us: local(): wg = lax.all_gather(wr, 'x', axis=2, tiled=False)]
    all_to_all x0 -> x2, waiting for transfers between devices: none -> 28.3 us  [the longest x1 17.5 us: local(): sl = lax.all_to_all(normed, 'x', 2, 0, tiled=True)]
    ppermute x0 -> x4, waiting for transfers between devices: none -> 20.7 us  [the longest x1 19.9 us: local(): ext = lax.ppermute(sl[:, :, :HEAD_WIDTH], COL, shift_pairs)]
    convert_element_type x1, local copies, waits for them, and re-layouts: 0.87 us -> 17 us  [local(): jnp.dot(tq, wg, preferred_element_type=jnp.float32).astype(jnp.bfloat16)]
    all_to_all x0 -> x1, blocking collectives: none -> 15.1 us  [local(): tq = lax.all_to_all(tq, 'x', 0, 0, tiled=True)]
    ppermute x0 -> x4, starting transfers between devices: none -> 13.7 us  [the longest x3 12.2 us: local(): got = [lax.ppermute(wp[:, j, :], COL, perms[j]) for j in range(3)]]
    reduce_sum x4 -> x1, other arithmetic: 12 us -> 0.28 us  [local(): jnp.sum(qv * qv, axis=-1)]
    psum x0 -> x1, blocking collectives: none -> 10.9 us  [local(): sums = lax.psum(sums, 'z')]
  transfers between devices with their start and end apart: 3 -> 9, of which waited for: 3 -> 7; matrix products, arithmetic and copies ran while one was open for 0% -> 3% of each run, Pallas kernels for 0% -> 0%
where the time goes in v1:
time: 316 us; the launch traced here: 315 us
  waiting for transfers between devices  174 us (55%)
  local copies, waits for them, and re-layouts  38.1 us (12%)
  matrix products  27 us (9%)
  blocking collectives  26 us (8%)
  starting transfers between devices  23.1 us (7%)
  between operations  21.3 us (7%)
  other arithmetic  5.5 us (2%)
    reduce_scatter x1, waiting for transfers between devices, local(): mine = lax.psum_scatter(part, ROW, scatter_dimension=0, tiled=True)[0]  68.1 us
    all_gather x1, waiting for transfers between devices, local(): wg = lax.all_gather(wr, 'x', axis=2, tiled=False)  34.2 us
    all_gather x1, waiting for transfers between devices, local(): tq = lax.all_gather(tq, 'z', axis=0, tiled=False)  22.3 us
    ppermute x1, waiting for transfers between devices, local(): ext = lax.ppermute(sl[:, :, :HEAD_WIDTH], COL, shift_pairs)  19.9 us
    all_to_all x1, waiting for transfers between devices, local(): sl = lax.all_to_all(normed, 'x', 2, 0, tiled=True)  17.5 us
    convert_element_type x1, local copies, waits for them, and re-layouts, local(): jnp.dot(tq, wg, preferred_element_type=jnp.float32).astype(jnp.bfloat16)  17 us
    all_to_all x1, blocking collectives, local(): tq = lax.all_to_all(tq, 'x', 0, 0, tiled=True)  15.1 us
    ppermute x3, starting transfers between devices, local(): got = [lax.ppermute(wp[:, j, :], COL, perms[j]) for j in range(3)]  12.2 us
  transfers between devices with their start and end apart: 9, of which 7 were waited for; matrix products, arithmetic and copies ran while one was open for 3% of the time, Pallas kernels for 0%

profile of v1, /device:TPU:8, one launch (start us, length us, event | category | flops | bytes accessed | tf_op | source)
XLA Modules:
  0.0 314.7 jit_solution(15563987543003411441)
XLA Ops:
  6.5 1.3 copy.45
  7.9 15.1 %all_to_all.25 = bf16[4,160,400]{2,1,0:T(8,128)(2,1)} all-to-all(bf16[4,160,400]{2,1,0:T(8,128)(2,1)S(1)} %bitcast.90), channel_id=1, replica_groups=mesh['y'=4,'k'=2,'x'=4,'z'=4] {'x'}, dimensions={0} | all-to-all | bytes 1024000 | tf_op jit(solution)/shard_map/all_to_all | solution.py:74
  23.0 0.2 copy.42
  23.3 2.7 collective-permute-start
  26.1 0.7 collective-permute-start.1
  26.8 8.8 %collective-permute-start.2 = (bf16[400,200]{0,1:T(8,128)(2,1)S(1)}, bf16[400,200]{0,1:T(8,128)(2,1)S(1)}, u32[]{:S(2)}, u32[]{:S(2)}) collective-permute-start(bf16[400,200]{0,1:T(8,128)(2,1)S(1)} %get-tuple-element.16), channel_id=1, source_target_pairs={{0,4},{1,1},{2,13},{3,10},{4,7},{5,0},{6,12},{7,9},{8,6},{9,3},{10... | collective-permute-start | bytes 480008 | tf_op jit(solution)/shard_map/ppermute | solution.py:62
  35.6 0.7 constant_dynamic-slice_fusion.2
  36.3 0.6 fusion.36
  40.9 0.8 collective-permute-done.2
  41.7 0.9 pad_maximum_fusion.2
  42.7 22.3 %all-gather.7.cloned.1.call-done = bf16[16,160,400]{2,1,0:T(8,128)(2,1)} async-done(((bf16[4,160,400]{2,1,0:T(8,128)(2,1)}), bf16[16,160,400]{2,1,0:T(8,128)(2,1)}) %all-gather.7.cloned.1.call-update) | async-done | bytes 2048016 | tf_op jit(solution)/shard_map/all_gather | solution.py:75
  65.0 2.0 copy.46
  67.0 34.2 %all-gather.5.cloned.1.call-done = bf16[400,3,800]{0,2,1:T(8,128)(2,1)} async-done(((bf16[400,3,200]{0,2,1:T(8,128)(2,1)}), bf16[400,3,800]{0,2,1:T(8,128)(2,1)}) %all-gather.5.cloned.1.call-update) | async-done | bytes 1920016 | tf_op jit(solution)/shard_map/all_gather | solution.py:70
  101.2 11.2 %fusion.3 = bf16[2560,2400]{0,1:T(8,128)(2,1)} fusion(bf16[400,2400]{0,1:T(8,128)(2,1)} %bitcast.102, bf16[2560,400]{1,0:T(8,128)(2,1)S(1)} %bitcast.89), kind=kOutput, calls=%fused_computation.6 | convolution fusion | flops 4921344000 | bytes 16256000 | tf_op jit(solution)/shard_map/dot_general | solution.py:78
  112.4 17.0 %copy.47 = bf16[2560,2400]{1,0:T(8,128)(2,1)} copy(bf16[2560,2400]{0,1:T(8,128)(2,1)} %fusion.3) | data formatting | bytes 24576000 | tf_op jit(solution)/shard_map/convert_element_type | solution.py:78
  129.4 0.8 dynamic_slice.19
  130.2 0.8 dynamic_slice.20
  131.0 68.1 %reduce-scatter.2.cloned.1.call-done = bf16[1,320,2400]{2,1,0:T(8,128)(2,1)} async-done(((bf16[8,320,2400]{2,1,0:T(8,128)(2,1)}), bf16[1,320,2400]{2,1,0:T(8,128)(2,1)}) %reduce-scatter.2.cloned.1.call-update) | async-done | bytes 1536016 | tf_op jit(solution)/shard_map/reduce_scatter | solution.py:81
  199.1 3.4 %copy.48 = bf16[1,320,2400]{1,2,0:T(8,128)(2,1)S(1)} copy(bf16[1,320,2400]{2,1,0:T(8,128)(2,1)} %reduce-scatter.2.cloned.1.call-done) | data formatting | bytes 3072000 | tf_op jit(solution)/shard_map/reduce_scatter | solution.py:81
  202.4 0.3 fusion.12
  202.7 0.1 slice.87
  202.8 10.9 %psum.7 = f32[320,2]{0,1:T(2,128)S(1)} all-reduce(f32[320,2]{0,1:T(2,128)S(1)} %pad_maximum_fusion.3), channel_id=1, replica_groups=mesh['y'=4,'k'=2,'x'=4,'z'=4] {'z'}, use_global_device_ids=true, to_apply=%region_3.4 | all-reduce | flops 640 | bytes 5120 | tf_op jit(solution)/shard_map/psum | solution.py:87
  213.8 0.3 fusion.14
  214.1 1.7 pad_maximum_fusion
  215.8 4.4 %all-to-all-start.1 = ((bf16[320,3,4,200]{0,3,1,2:T(8,128)(2,1)}), bf16[320,3,4,200]{0,3,1,2:T(8,128)(2,1)S(1)}, u32[]{:S(2)}, u32[]{:S(2)}) async-start(bf16[320,3,4,200]{0,3,1,2:T(8,128)(2,1)} %pad_maximum_fusion), calls=%async_computation.2 | async-start | bytes 3686400 | tf_op jit(solution)/shard_map/all_to_all | solution.py:96
  220.2 0.7 constant_dynamic-slice_fusion.1
  220.9 0.6 fusion.35
  224.1 0.1 reshape_squeeze.6
  224.2 0.1 eq.55
  225.6 17.5 %all-to-all-done.1 = bf16[320,3,4,200]{0,3,1,2:T(8,128)(2,1)S(1)} async-done(((bf16[320,3,4,200]{0,3,1,2:T(8,128)(2,1)}), bf16[320,3,4,200]{0,3,1,2:T(8,128)(2,1)S(1)}, u32[]{:S(2)}, u32[]{:S(2)}) %all-to-all-start.1) | async-done | bytes 1536032 | tf_op jit(solution)/shard_map/all_to_all | solution.py:96
  243.2 2.0 copy.52
  245.2 3.4 %reshape.128 = bf16[1280,3,200]{0,2,1:T(8,128)(2,1)S(1)} reshape(bf16[4,320,3,1,200]{1,0,4,2,3:T(4,128)(2,1)} %copy.52) | data formatting | bytes 3072000 | tf_op jit(solution)/shard_map/reshape | solution.py:97
  248.6 0.1 slice.88
  248.6 1.5 collective-permute-start.3
  250.1 2.2 broadcast_compare_fusion
  252.3 0.1 constant_dynamic-update-slice_fusion.1
  252.4 19.9 %collective-permute-done.3 = bf16[1280,3,128]{0,2,1:T(8,128)(2,1)S(1)} collective-permute-done((bf16[1280,3,128]{0,2,1:T(8,128)(2,1)S(1)}, bf16[1280,3,128]{0,2,1:T(8,128)(2,1)S(1)}, u32[]{:S(2)}, u32[]{:S(2)}) %collective-permute-start.3) | collective-permute-done | bytes 983072 | tf_op jit(solution)/shard_map/ppermute | solution.py:98
  272.3 0.1 constant_dynamic-update-slice_fusion
  272.4 0.5 constant_dynamic-slice_fusion.3
  272.9 0.7 copy.53
  273.5 0.7 copy.54
  274.2 10.3 %fusion.37 = (f32[2,1280]{1,0:T(2,128)S(1)}, bf16[2,1280,1280]{1,2,0:T(8,128)(2,1)}) fusion(pred[1280,1280]{0,1:T(8,128)(4,1)} %broadcast_compare_fusion, bf16[1280,3,1,128]{3,0,2,1:T(8,128)(2,1)S(1)} %bitcast.96, bf16[1280,3,1,128]{3,0,2,1:T(8,128)(2,1)S(1)} %bitcast.98), kind=kOutput, calls=%fused_computation.61 | convolution fusion | flops 859178240 | bytes 13772800 | tf_op jit(solution)/shard_map/sub | solution.py:115
  284.5 5.6 %fusion.9 = bf16[2,1280,128]{2,1,0:T(8,128)(2,1)S(1)} fusion(bf16[2,1280,1280]{1,2,0:T(8,128)(2,1)} %get-tuple-element.24, bf16[1280,3,1,128]{3,0,2,1:T(8,128)(2,1)S(1)} %bitcast.99, bf16[1280,3,1,128]{3,0,2,1:T(8,128)(2,1)S(1)} %bitcast.97, f32[2,1280]{1,0:T(2,128)S(1)} %get-tuple-element.23), kind=kOutput, calls=%fused_computation.12 | convolution fusion | flops 839843840 | bytes 9185280 | tf_op jit(solution)/shard_map/hqk,khd->hqd/dot_general | solution.py:118
  290.1 0.9 copy.56
  291.0 4.9 %all-to-all-start.2 = ((bf16[16,80,2,128]{3,1,2,0:T(8,128)(2,1)}), bf16[16,80,2,128]{3,1,2,0:T(8,128)(2,1)S(1)}, u32[]{:S(2)}, u32[]{:S(2)}) async-start(bf16[16,80,2,128]{3,1,2,0:T(8,128)(2,1)} %bitcast.39), calls=%async_computation.3 | async-start | bytes 1310720 | tf_op jit(solution)/shard_map/all_to_all | solution.py:124
  296.0 10.8 %all-to-all-done.2 = bf16[16,80,2,128]{3,1,2,0:T(8,128)(2,1)S(1)} async-done(((bf16[16,80,2,128]{3,1,2,0:T(8,128)(2,1)}), bf16[16,80,2,128]{3,1,2,0:T(8,128)(2,1)S(1)}, u32[]{:S(2)}, u32[]{:S(2)}) %all-to-all-start.2) | async-done | bytes 655392 | tf_op jit(solution)/shard_map/all_to_all | solution.py:124
  306.7 0.6 gather_fusion
  307.4 0.8 copy_bitcast_fusion
  (24 shorter events, 0.3 us)
Async XLA Ops:
  6.5 16.5 %copy-start = (bf16[400,600]{1,0:T(8,128)(2,1)S(1)}, bf16[400,600]{1,0:T(8,128)(2,1)}, u32[]{:S(2)}) copy-start(bf16[400,600]{1,0:T(8,128)(2,1)} %param.9) | copy-start | bytes 1440004
  6.5 58.5 %all-gather.7.cloned.1.call-start = ((), (), s32[]{:S(2)}) async-start(), calls=%async_computation.6 | async-start | bytes 3276800 | tf_op jit(solution)/shard_map/all_gather | solution.py:75
  23.0 78.3 %all-gather.5.cloned.1.call-start = ((), (), s32[]{:S(2)}) async-start(), calls=%async_computation.5 | async-start | bytes 3072000 | tf_op jit(solution)/shard_map/all_gather | solution.py:70
  23.3 17.5 %collective-permute-start = (bf16[400,200]{0,1:T(8,128)(2,1)S(1)}, bf16[400,200]{0,1:T(8,128)(2,1)S(1)}, u32[]{:S(2)}, u32[]{:S(2)}) collective-permute-start(bf16[400,200]{0,1:T(8,128)(2,1)S(1)} %get-tuple-element.18), channel_id=1, source_target_pairs={{0,8},{1,5},{2,2},{3,14},{4,11},{5,4},{6,1},{7,13},{8,10},{9,7},{1... | collective-permute-start | bytes 480008 | tf_op jit(solution)/shard_map/ppermute | solution.py:62
  26.1 14.8 %collective-permute-start.1 = (bf16[400,200]{0,1:T(8,128)(2,1)S(1)}, bf16[400,200]{0,1:T(8,128)(2,1)S(1)}, u32[]{:S(2)}, u32[]{:S(2)}) collective-permute-start(bf16[400,200]{0,1:T(8,128)(2,1)S(1)} %get-tuple-element.17), channel_id=1, source_target_pairs={{0,0},{1,12},{2,9},{3,6},{4,3},{5,15},{6,8},{7,5},{8,2},{9,14},{10... | collective-permute-start | bytes 480008 | tf_op jit(solution)/shard_map/ppermute | solution.py:62
  26.8 14.9 %collective-permute-start.2 = (bf16[400,200]{0,1:T(8,128)(2,1)S(1)}, bf16[400,200]{0,1:T(8,128)(2,1)S(1)}, u32[]{:S(2)}, u32[]{:S(2)}) collective-permute-start(bf16[400,200]{0,1:T(8,128)(2,1)S(1)} %get-tuple-element.16), channel_id=1, source_target_pairs={{0,4},{1,1},{2,13},{3,10},{4,7},{5,0},{6,12},{7,9},{8,6},{9,3},{10... | collective-permute-start | bytes 480008 | tf_op jit(solution)/shard_map/ppermute | solution.py:62
  42.7 156.4 %reduce-scatter.2.cloned.1.call-start = ((), (), s32[]{:S(2)}) async-start(), calls=%async_computation.4 | async-start | bytes 14008320 | tf_op jit(solution)/shard_map/reduce_scatter | solution.py:81
  215.8 8.3 %copy-start.1 = (s32[1,1280]{1,0:T(1,128)S(1)}, s32[1,1280]{1,0:T(1,128)}, u32[]{:S(2)}) copy-start(s32[1,1280]{1,0:T(1,128)} %param.12) | copy-start | bytes 15364
  215.8 27.4 %all-to-all-start.1 = ((bf16[320,3,4,200]{0,3,1,2:T(8,128)(2,1)}), bf16[320,3,4,200]{0,3,1,2:T(8,128)(2,1)S(1)}, u32[]{:S(2)}, u32[]{:S(2)}) async-start(bf16[320,3,4,200]{0,3,1,2:T(8,128)(2,1)} %pad_maximum_fusion), calls=%async_computation.2 | async-start | bytes 3686400 | tf_op jit(solution)/shard_map/all_to_all | solution.py:96
  248.6 23.7 %collective-permute-start.3 = (bf16[1280,3,128]{0,2,1:T(8,128)(2,1)S(1)}, bf16[1280,3,128]{0,2,1:T(8,128)(2,1)S(1)}, u32[]{:S(2)}, u32[]{:S(2)}) collective-permute-start(bf16[1280,3,128]{0,2,1:T(8,128)(2,1)S(1)} %slice.88), channel_id=1, source_target_pairs={{4,0},{8,4},{12,8},{1,12},{5,1},{9,5},{13,9},{2,13},{6,2},{10,6},{... | collective-permute-start | bytes 2949128 | tf_op jit(solution)/shard_map/ppermute | solution.py:98
  290.1 5.9 %copy-start.2 = (s32[25]{0:T(128)S(1)}, s32[25]{0:T(128)}, u32[]{:S(2)}) copy-start(s32[25]{0:T(128)} %constant.78) | copy-start | bytes 304
  291.0 15.7 %all-to-all-start.2 = ((bf16[16,80,2,128]{3,1,2,0:T(8,128)(2,1)}), bf16[16,80,2,128]{3,1,2,0:T(8,128)(2,1)S(1)}, u32[]{:S(2)}, u32[]{:S(2)}) async-start(bf16[16,80,2,128]{3,1,2,0:T(8,128)(2,1)} %bitcast.39), calls=%async_computation.3 | async-start | bytes 1310720 | tf_op jit(solution)/shard_map/all_to_all | solution.py:124
Sparse Core Ops, SparseCore 0:
  23.1 41.8 all-gather.6
  66.7 34.5 all-gather.4
  129.5 69.4 reduce-scatter.1

commit v2 on v1

--- a/solution.py
+++ b/solution.py
@@ -8,6 +8,35 @@
 HEAD_WIDTH = 128
 ROW = ("y", "k")
 COL = ("x", "z")
+
+
+def shift_gather(v, axis, n, me, dim):
+    shape = list(v.shape)
+    shape.insert(dim, n)
+    out = jnp.zeros(shape, v.dtype)
+    out = lax.dynamic_update_index_in_dim(out, v, me, dim)
+    for s in range(1, n):
+        got = lax.ppermute(v, axis, [(i, (i + s) % n) for i in range(n)])
+        out = lax.dynamic_update_index_in_dim(out, got, (me - s) % n, dim)
+    return out
+
+
+def shift_all_to_all(v, axis, n, me):
+    out = jnp.zeros_like(v)
+    out = lax.dynamic_update_index_in_dim(out, lax.dynamic_index_in_dim(v, me, 0, False), me, 0)
+    for s in range(1, n):
+        piece = lax.dynamic_index_in_dim(v, (me + s) % n, 0, False)
+        got = lax.ppermute(piece, axis, [(i, (i + s) % n) for i in range(n)])
+        out = lax.dynamic_update_index_in_dim(out, got, (me - s) % n, 0)
+    return out
+
+
+def butterfly_sum(v, axis, n):
+    step = 1
+    while step < n:
+        v = v + lax.ppermute(v, axis, [(i, i ^ step) for i in range(n)])
+        step *= 2
+    return v
 
 
 def build_local(nx, nz):
@@ -67,24 +96,24 @@
             acc = jnp.where(reg[2] == s, got[2], acc)
             wr.append(acc)
         wr = jnp.stack(wr, axis=1)
-        wg = lax.all_gather(wr, "x", axis=2, tiled=False)
+        wg = shift_gather(wr, "x", nx, x, 2)
         wg = wg.reshape(feat_blk, 3 * nx * piece)
 
         tq = tokens.reshape(nx, quarter, feat_blk)
-        tq = lax.all_to_all(tq, "x", 0, 0, tiled=True)
-        tq = lax.all_gather(tq, "z", axis=0, tiled=False)
-        tq = jnp.transpose(tq, (1, 0, 2, 3)).reshape(nc * quarter, feat_blk)
+        tq = shift_all_to_all(tq, "x", nx, x)
+        tq = shift_gather(tq, "z", nz, z, 1)
+        n_packs = nc // 2
+        tq = tq.reshape(n_packs, 2 * quarter, feat_blk)
 
-        part = jnp.dot(tq, wg, preferred_element_type=jnp.float32).astype(jnp.bfloat16)
-        n_packs = nc // 2
-        part = part.reshape(n_packs, 2 * quarter, 3 * nx * piece)
+        part = jnp.einsum("ptf,fc->ptc", tq, wg, preferred_element_type=jnp.float32)
+        part = part.astype(jnp.bfloat16)
         mine = lax.psum_scatter(part, ROW, scatter_dimension=0, tiled=True)[0]
         mine = mine.reshape(2 * quarter, 3, nx * piece)
 
         qv = mine[:, 0, :].astype(jnp.float32)
         kv = mine[:, 1, :].astype(jnp.float32)
         sums = jnp.stack([jnp.sum(qv * qv, axis=-1), jnp.sum(kv * kv, axis=-1)], axis=-1)
-        sums = lax.psum(sums, "z")
+        sums = butterfly_sum(sums, "z", nz)
         rs = lax.rsqrt(sums / width + 1e-06)
         qg = lax.dynamic_slice_in_dim(q_gain, z * nx * piece, nx * piece)
         kg = lax.dynamic_slice_in_dim(k_gain, z * nx * piece, nx * piece)

time: 316 us -> 312 us (0.987)
  waiting for transfers between devices: 174 us -> 147 us
  starting transfers between devices: 23.1 us -> 49.4 us
  blocking collectives: 26 us -> 0 us
  local copies, waits for them, and re-layouts: 38.1 us -> 58.2 us
    all_gather x2 -> x0, waiting for transfers between devices: 56.5 us -> none  [the longest x1 34.2 us: local(): wg = lax.all_gather(wr, 'x', axis=2, tiled=False)]
    ppermute x0 -> x11, waiting for transfers between devices: none -> 30.5 us  [the longest x6 20.4 us: shift_gather(): got = lax.ppermute(v, axis, [(i, (i + s) % n) for i in range(n)])]
    dynamic_update_slice x0 -> x11, local copies, waits for them, and re-layouts: none -> 30 us  [the longest x7 29.9 us: shift_gather(): out = lax.dynamic_update_index_in_dim(out, got, (me - s) % n, dim)]
    ppermute x0 -> x11, starting transfers between devices: none -> 23.4 us  [the longest x6 14.7 us: shift_gather(): got = lax.ppermute(v, axis, [(i, (i + s) % n) for i in range(n)])]
    convert_element_type x1 -> x0, local copies, waits for them, and re-layouts: 17 us -> none  [local(): jnp.dot(tq, wg, preferred_element_type=jnp.float32).astype(jnp.bfloat16)]
    all_to_all x1 -> x0, blocking collectives: 15.1 us -> none  [local(): tq = lax.all_to_all(tq, 'x', 0, 0, tiled=True)]
    psum x1 -> x0, blocking collectives: 10.9 us -> none  [local(): sums = lax.psum(sums, 'z')]
    broadcast_in_dim x0 -> x4, local copies, waits for them, and re-layouts: none -> 4.9 us  [the longest x1 2.98 us: shift_gather(): out = lax.dynamic_update_index_in_dim(out, got, (me - s) % n, dim)]
  transfers between devices with their start and end apart: 9 -> 18, of which waited for: 7 -> 12; matrix products, arithmetic and copies ran while one was open for 3% -> 6% of each run, Pallas kernels for 0% -> 0%
where the time goes in v2:
time: 312 us; the launch traced here: 309 us
  waiting for transfers between devices  147 us (47%)
  local copies, waits for them, and re-layouts  58.2 us (19%)
  starting transfers between devices  49.4 us (16%)
  matrix products  27.5 us (9%)
  between operations  21.8 us (7%)
  other arithmetic  5.11 us (2%)
    reduce_scatter x1, waiting for transfers between devices, local(): mine = lax.psum_scatter(part, ROW, scatter_dimension=0, tiled=True)[0]  67.3 us
    dynamic_update_slice x7, local copies, waits for them, and re-layouts, shift_gather(): out = lax.dynamic_update_index_in_dim(out, got, (me - s) % n, dim)  29.9 us
    ppermute x6, waiting for transfers between devices, shift_gather(): got = lax.ppermute(v, axis, [(i, (i + s) % n) for i in range(n)])  20.4 us
    ppermute x1, waiting for transfers between devices, local(): ext = lax.ppermute(sl[:, :, :HEAD_WIDTH], COL, shift_pairs)  20.4 us
    all_to_all x1, waiting for transfers between devices, local(): sl = lax.all_to_all(normed, 'x', 2, 0, tiled=True)  17.8 us
    ppermute x6, starting transfers between devices, shift_gather(): got = lax.ppermute(v, axis, [(i, (i + s) % n) for i in range(n)])  14.7 us
    ppermute x3, starting transfers between devices, local(): got = [lax.ppermute(wp[:, j, :], COL, perms[j]) for j in range(3)]  13.8 us
    dot_general x1, matrix products, local(): part = jnp.einsum('ptf,fc->ptc', tq, wg, preferred_element_type=jnp.float32)  11.7 us
  transfers between devices with their start and end apart: 18, of which 12 were waited for; matrix products, arithmetic and copies ran while one was open for 6% of the time, Pallas kernels for 0%

profile of v2, /device:TPU:8, one launch (start us, length us, event | category | flops | bytes accessed | tf_op | source)
XLA Modules:
  0.0 308.8 jit_solution(7129773505309836882)
XLA Ops:
  6.5 1.3 copy.58
  7.9 4.9 %collective-permute-start.6 = (bf16[400,200]{0,1:T(8,128)(2,1)S(1)}, bf16[400,200]{0,1:T(8,128)(2,1)S(1)}, u32[]{:S(2)}, u32[]{:S(2)}) collective-permute-start(bf16[400,200]{0,1:T(8,128)(2,1)S(1)} %get-tuple-element.22), channel_id=1, source_target_pairs={{0,8},{1,5},{2,2},{3,14},{4,11},{5,4},{6,1},{7,13},{8,10},{9,7},{1... | collective-permute-start | bytes 480008 | tf_op jit(solution)/shard_map/ppermute | solution.py:91
  12.9 0.7 collective-permute-start.7
  13.5 8.2 %collective-permute-start.8 = (bf16[400,200]{0,1:T(8,128)(2,1)S(1)}, bf16[400,200]{0,1:T(8,128)(2,1)S(1)}, u32[]{:S(2)}, u32[]{:S(2)}) collective-permute-start(bf16[400,200]{0,1:T(8,128)(2,1)S(1)} %get-tuple-element.20), channel_id=1, source_target_pairs={{0,4},{1,1},{2,13},{3,10},{4,7},{5,0},{6,12},{7,9},{8,6},{9,3},{10... | collective-permute-start | bytes 480008 | tf_op jit(solution)/shard_map/ppermute | solution.py:91
  22.3 3.3 %collective-permute-start.1 = (bf16[160,400]{1,0:T(8,128)(2,1)S(1)}, bf16[160,400]{1,0:T(8,128)(2,1)S(1)}, u32[]{:S(2)}, u32[]{:S(2)}) collective-permute-start(bf16[160,400]{1,0:T(8,128)(2,1)S(1)} %get-tuple-element.14), channel_id=1, source_target_pairs={{0,8},{4,12},{8,0},{12,4},{1,9},{5,13},{9,1},{13,5},{2,10},{6,14},... | collective-permute-start | bytes 384008 | tf_op jit(solution)/shard_map/ppermute | solution.py:29
  25.6 0.7 constant_dynamic-slice_fusion.2
  30.9 2.9 collective-permute-done
  33.8 5.3 %collective-permute-done.2 = bf16[160,400]{1,0:T(8,128)(2,1)S(1)} collective-permute-done((bf16[160,400]{1,0:T(8,128)(2,1)S(1)}, bf16[160,400]{1,0:T(8,128)(2,1)S(1)}, u32[]{:S(2)}, u32[]{:S(2)}) %collective-permute-start.2) | collective-permute-done | bytes 128032 | tf_op jit(solution)/shard_map/ppermute | solution.py:29
  39.1 7.4 %collective-permute-start.3 = (bf16[4,160,400]{2,1,0:T(8,128)(2,1)S(1)}, bf16[4,160,400]{2,1,0:T(8,128)(2,1)S(1)}, u32[]{:S(2)}, u32[]{:S(2)}) collective-permute-start(bf16[4,160,400]{2,1,0:T(8,128)(2,1)S(1)} %bitcast_dynamic-update-slice_fusion.7), channel_id=1, source_target_pairs={{0,1},{1,2},{2,3},{3,0},{4,5},{5,6},{6,7},{7,4},{8,9},{9,10},{10,1... | collective-permute-start | bytes 1536008 | tf_op jit(solution)/shard_map/ppermute | solution.py:19
  46.8 2.8 collective-permute-start.5
  49.7 0.9 pad_maximum_fusion.2
  50.6 3.0 collective-permute-start.10
  53.6 1.6 broadcast_in_dim.92
  55.2 0.9 bitcast_dynamic-update-slice_fusion.6
  56.1 5.5 %collective-permute-done.3 = bf16[4,160,400]{2,1,0:T(8,128)(2,1)S(1)} collective-permute-done((bf16[4,160,400]{2,1,0:T(8,128)(2,1)S(1)}, bf16[4,160,400]{2,1,0:T(8,128)(2,1)S(1)}, u32[]{:S(2)}, u32[]{:S(2)}) %collective-permute-start.3) | collective-permute-done | bytes 512032 | tf_op jit(solution)/shard_map/ppermute | solution.py:19
  61.6 1.5 collective-permute-start.11
  63.2 10.3 %collective-permute-done.4 = bf16[4,160,400]{2,1,0:T(8,128)(2,1)S(1)} collective-permute-done((bf16[4,160,400]{2,1,0:T(8,128)(2,1)S(1)}, bf16[4,160,400]{2,1,0:T(8,128)(2,1)S(1)}, u32[]{:S(2)}, u32[]{:S(2)}) %collective-permute-start.4) | collective-permute-done | bytes 512032 | tf_op jit(solution)/shard_map/ppermute | solution.py:19
  73.5 0.8 collective-permute-done.5
  74.4 0.9 bitcast_dynamic-update-slice_fusion.5
  75.4 3.8 %collective-permute-done.10 = bf16[400,3,200]{0,2,1:T(8,128)(2,1)S(1)} collective-permute-done((bf16[400,3,200]{0,2,1:T(8,128)(2,1)}, bf16[400,3,200]{0,2,1:T(8,128)(2,1)S(1)}, u32[]{:S(2)}, u32[]{:S(2)}) %collective-permute-start.10) | collective-permute-done | bytes 480032 | tf_op jit(solution)/shard_map/ppermute | solution.py:19
  79.2 0.9 bitcast_dynamic-update-slice_fusion.4
  80.1 4.7 %copy.61 = bf16[400,3,4,200]{3,2,1,0:T(4,128)(2,1)S(1)} copy(bf16[400,3,4,200]{0,3,1,2:T(8,128)(2,1)} %bitcast_dynamic-update-slice_fusion.4) | data formatting | bytes 3840000 | tf_op jit(solution)/shard_map/jit(dynamic_update_index_in_dim)/dynamic_update_slice | solution.py:20
  84.8 3.0 copy.62
  87.8 23.2 %dynamic_update_slice.50 = bf16[400,3,4,200]{3,2,1,0:T(4,128)(2,1)S(1)} dynamic-update-slice(bf16[400,3,4,200]{3,2,1,0:T(4,128)(2,1)S(1)} %copy.61, bf16[400,3,1,200]{3,2,1,0:T(2,128)(2,1)} %copy.62, s32[]{:T(128)} %constant.142.clone.1, s32[]{:T(128)} %constant.142.clone.1, s32[]{:T(128)S(6)} %select_n.172, s32[]{:T(128)} %constant.142.clone.1) | dynamic-update-slice | bytes 960004 | tf_op jit(solution)/shard_map/jit(dynamic_update_index_in_dim)/dynamic_update_slice | solution.py:20
  111.0 2.6 reshape.137
  113.7 11.7 %convolution_convert_fusion = bf16[8,320,2400]{2,1,0:T(8,128)(2,1)} fusion(bf16[8,320,400]{2,1,0:T(8,128)(2,1)} %bitcast.107, bf16[400,2400,1]{1,0,2:T(8,128)(2,1)} %reshape.137), kind=kOutput, calls=%fused_computation.6 | convolution fusion | flops 4921344000 | bytes 16256000 | tf_op jit(solution)/shard_map/ptf,fc->ptc/dot_general | solution.py:108
  125.4 67.3 %reduce-scatter.2.cloned.1.call-done = bf16[1,320,2400]{2,1,0:T(8,128)(2,1)} async-done(((bf16[8,320,2400]{2,1,0:T(8,128)(2,1)}), bf16[1,320,2400]{2,1,0:T(8,128)(2,1)}) %reduce-scatter.2.cloned.1.call-update) | async-done | bytes 1536016 | tf_op jit(solution)/shard_map/reduce_scatter | solution.py:110
  192.7 3.4 %copy.64 = bf16[1,320,2400]{1,2,0:T(8,128)(2,1)S(1)} copy(bf16[1,320,2400]{2,1,0:T(8,128)(2,1)} %reduce-scatter.2.cloned.1.call-done) | data formatting | bytes 3072000 | tf_op jit(solution)/shard_map/reduce_scatter | solution.py:110
  196.4 1.8 collective-permute-start.12
  198.2 1.8 collective-permute-done.12
  200.1 3.4 %collective-permute-start.13 = (f32[320,2]{0,1:T(2,128)S(1)}, f32[320,2]{0,1:T(2,128)S(1)}, u32[]{:S(2)}, u32[]{:S(2)}) collective-permute-start(f32[320,2]{0,1:T(2,128)S(1)} %fusion.28), channel_id=1, source_target_pairs={{0,2},{1,3},{2,0},{3,1},{4,6},{5,7},{6,4},{7,5},{8,10},{9,11},{10,... | collective-permute-start | bytes 7688 | tf_op jit(solution)/shard_map/ppermute | solution.py:37
  203.5 0.8 dynamic_slice.36
  204.3 0.8 dynamic_slice.37
  206.0 1.4 copy.65
  207.5 4.8 %all-to-all-start = ((bf16[320,3,4,200]{0,3,1,2:T(8,128)(2,1)}), bf16[320,3,4,200]{0,3,1,2:T(8,128)(2,1)S(1)}, u32[]{:S(2)}, u32[]{:S(2)}) async-start(bf16[320,3,4,200]{0,3,1,2:T(8,128)(2,1)} %copy.65), calls=%async_computation.1 | async-start | bytes 3686400 | tf_op jit(solution)/shard_map/all_to_all | solution.py:125
  212.2 0.7 constant_dynamic-slice_fusion.1
  217.8 17.8 %all-to-all-done = bf16[320,3,4,200]{0,3,1,2:T(8,128)(2,1)S(1)} async-done(((bf16[320,3,4,200]{0,3,1,2:T(8,128)(2,1)}), bf16[320,3,4,200]{0,3,1,2:T(8,128)(2,1)S(1)}, u32[]{:S(2)}, u32[]{:S(2)}) %all-to-all-start) | async-done | bytes 1536032 | tf_op jit(solution)/shard_map/all_to_all | solution.py:125
  235.5 2.0 copy.66
  237.5 3.4 %reshape.124 = bf16[1280,3,200]{0,2,1:T(8,128)(2,1)S(1)} reshape(bf16[4,320,3,1,200]{1,0,4,2,3:T(4,128)(2,1)} %copy.66) | data formatting | bytes 3072000 | tf_op jit(solution)/shard_map/reshape | solution.py:126
  241.0 1.3 collective-permute-start.14
  242.3 2.1 broadcast_compare_fusion
  244.5 20.4 %collective-permute-done.14 = bf16[1280,3,128]{0,2,1:T(8,128)(2,1)S(1)} collective-permute-done((bf16[1280,3,128]{0,2,1:T(8,128)(2,1)S(1)}, bf16[1280,3,128]{0,2,1:T(8,128)(2,1)S(1)}, u32[]{:S(2)}, u32[]{:S(2)}) %collective-permute-start.14) | collective-permute-done | bytes 983072 | tf_op jit(solution)/shard_map/ppermute | solution.py:127
  266.8 10.2 %fusion.37 = (f32[2,1280]{1,0:T(2,128)S(1)}, bf16[2,1280,1280]{1,2,0:T(8,128)(2,1)}) fusion(pred[1280,1280]{0,1:T(8,128)(4,1)} %broadcast_compare_fusion, bf16[1280,3,1,128]{3,0,2,1:T(8,128)(2,1)S(1)} %bitcast.114, bf16[1280,3,1,128]{3,0,2,1:T(8,128)(2,1)S(1)} %bitcast.116), kind=kOutput, calls=%fused_computation.75 | convolution fusion | flops 859178240 | bytes 13772800 | tf_op jit(solution)/shard_map/sub | solution.py:144
  277.1 5.6 %fusion.8 = bf16[2,1280,128]{2,1,0:T(8,128)(2,1)S(1)} fusion(bf16[2,1280,1280]{1,2,0:T(8,128)(2,1)} %get-tuple-element.28, bf16[1280,3,1,128]{3,0,2,1:T(8,128)(2,1)S(1)} %bitcast.117, bf16[1280,3,1,128]{3,0,2,1:T(8,128)(2,1)S(1)} %bitcast.115, f32[2,1280]{1,0:T(2,128)S(1)} %get-tuple-element.27), kind=kOutput, calls=%fused_computation.11 | convolution fusion | flops 839843840 | bytes 9185280 | tf_op jit(solution)/shard_map/hqk,khd->hqd/dot_general | solution.py:147
  282.7 0.9 copy.70
  283.5 6.2 %all-to-all-start.1 = ((bf16[16,80,2,128]{3,1,2,0:T(8,128)(2,1)}), bf16[16,80,2,128]{3,1,2,0:T(8,128)(2,1)S(1)}, u32[]{:S(2)}, u32[]{:S(2)}) async-start(bf16[16,80,2,128]{3,1,2,0:T(8,128)(2,1)} %bitcast.48), calls=%async_computation.2 | async-start | bytes 1310720 | tf_op jit(solution)/shard_map/all_to_all | solution.py:153
  289.7 10.8 %all-to-all-done.1 = bf16[16,80,2,128]{3,1,2,0:T(8,128)(2,1)S(1)} async-done(((bf16[16,80,2,128]{3,1,2,0:T(8,128)(2,1)}), bf16[16,80,2,128]{3,1,2,0:T(8,128)(2,1)S(1)}, u32[]{:S(2)}, u32[]{:S(2)}) %all-to-all-start.1) | async-done | bytes 655392 | tf_op jit(solution)/shard_map/all_to_all | solution.py:153
  301.2 0.8 copy_bitcast_fusion
  (58 shorter events, 6.5 us)
Async XLA Ops:
  6.5 15.3 %copy-start.1 = (bf16[640,400]{0,1:T(8,128)(2,1)S(1)}, bf16[640,400]{0,1:T(8,128)(2,1)}, u32[]{:S(2)}) copy-start(bf16[640,400]{0,1:T(8,128)(2,1)} %param.8) | copy-start | bytes 1536004
  6.5 186.2 %reduce-scatter.2.cloned.1.call-start = ((), (), s32[]{:S(2)}) async-start(), calls=%async_computation.3 | async-start | bytes 14008320 | tf_op jit(solution)/shard_map/reduce_scatter | solution.py:110
  7.9 38.9 %collective-permute-start.6 = (bf16[400,200]{0,1:T(8,128)(2,1)S(1)}, bf16[400,200]{0,1:T(8,128)(2,1)S(1)}, u32[]{:S(2)}, u32[]{:S(2)}) collective-permute-start(bf16[400,200]{0,1:T(8,128)(2,1)S(1)} %get-tuple-element.22), channel_id=1, source_target_pairs={{0,8},{1,5},{2,2},{3,14},{4,11},{5,4},{6,1},{7,13},{8,10},{9,7},{1... | collective-permute-start | bytes 480008 | tf_op jit(solution)/shard_map/ppermute | solution.py:91
  12.9 36.8 %collective-permute-start.7 = (bf16[400,200]{0,1:T(8,128)(2,1)S(1)}, bf16[400,200]{0,1:T(8,128)(2,1)S(1)}, u32[]{:S(2)}, u32[]{:S(2)}) collective-permute-start(bf16[400,200]{0,1:T(8,128)(2,1)S(1)} %get-tuple-element.21), channel_id=1, source_target_pairs={{0,0},{1,12},{2,9},{3,6},{4,3},{5,15},{6,8},{7,5},{8,2},{9,14},{10... | collective-permute-start | bytes 480008 | tf_op jit(solution)/shard_map/ppermute | solution.py:91
  13.5 36.1 %collective-permute-start.8 = (bf16[400,200]{0,1:T(8,128)(2,1)S(1)}, bf16[400,200]{0,1:T(8,128)(2,1)S(1)}, u32[]{:S(2)}, u32[]{:S(2)}) collective-permute-start(bf16[400,200]{0,1:T(8,128)(2,1)S(1)} %get-tuple-element.20), channel_id=1, source_target_pairs={{0,4},{1,1},{2,13},{3,10},{4,7},{5,0},{6,12},{7,9},{8,6},{9,3},{10... | collective-permute-start | bytes 480008 | tf_op jit(solution)/shard_map/ppermute | solution.py:91
  22.2 11.5 %collective-permute-start = (bf16[160,400]{1,0:T(8,128)(2,1)S(1)}, bf16[160,400]{1,0:T(8,128)(2,1)S(1)}, u32[]{:S(2)}, u32[]{:S(2)}) collective-permute-start(bf16[160,400]{1,0:T(8,128)(2,1)S(1)} %get-tuple-element.15), channel_id=1, source_target_pairs={{0,4},{4,8},{8,12},{12,0},{1,5},{5,9},{9,13},{13,1},{2,6},{6,10},{... | collective-permute-start | bytes 384008 | tf_op jit(solution)/shard_map/ppermute | solution.py:29
  22.3 11.5 %collective-permute-start.1 = (bf16[160,400]{1,0:T(8,128)(2,1)S(1)}, bf16[160,400]{1,0:T(8,128)(2,1)S(1)}, u32[]{:S(2)}, u32[]{:S(2)}) collective-permute-start(bf16[160,400]{1,0:T(8,128)(2,1)S(1)} %get-tuple-element.14), channel_id=1, source_target_pairs={{0,8},{4,12},{8,0},{12,4},{1,9},{5,13},{9,1},{13,5},{2,10},{6,14},... | collective-permute-start | bytes 384008 | tf_op jit(solution)/shard_map/ppermute | solution.py:29
  33.7 5.3 %collective-permute-start.2 = (bf16[160,400]{1,0:T(8,128)(2,1)S(1)}, bf16[160,400]{1,0:T(8,128)(2,1)S(1)}, u32[]{:S(2)}, u32[]{:S(2)}) collective-permute-start(bf16[160,400]{1,0:T(8,128)(2,1)S(1)} %get-tuple-element.13), channel_id=1, source_target_pairs={{0,12},{4,0},{8,4},{12,8},{1,13},{5,1},{9,5},{13,9},{2,14},{6,2},{... | collective-permute-start | bytes 384008 | tf_op jit(solution)/shard_map/ppermute | solution.py:29
  39.1 22.5 %collective-permute-start.3 = (bf16[4,160,400]{2,1,0:T(8,128)(2,1)S(1)}, bf16[4,160,400]{2,1,0:T(8,128)(2,1)S(1)}, u32[]{:S(2)}, u32[]{:S(2)}) collective-permute-start(bf16[4,160,400]{2,1,0:T(8,128)(2,1)S(1)} %bitcast_dynamic-update-slice_fusion.7), channel_id=1, source_target_pairs={{0,1},{1,2},{2,3},{3,0},{4,5},{5,6},{6,7},{7,4},{8,9},{9,10},{10,1... | collective-permute-start | bytes 1536008 | tf_op jit(solution)/shard_map/ppermute | solution.py:19
  46.5 27.0 %collective-permute-start.4 = (bf16[4,160,400]{2,1,0:T(8,128)(2,1)S(1)}, bf16[4,160,400]{2,1,0:T(8,128)(2,1)S(1)}, u32[]{:S(2)}, u32[]{:S(2)}) collective-permute-start(bf16[4,160,400]{2,1,0:T(8,128)(2,1)S(1)} %bitcast_dynamic-update-slice_fusion.7), channel_id=1, source_target_pairs={{0,2},{1,3},{2,0},{3,1},{4,6},{5,7},{6,4},{7,5},{8,10},{9,11},{10,... | collective-permute-start | bytes 1536008 | tf_op jit(solution)/shard_map/ppermute | solution.py:19
  46.8 27.5 %collective-permute-start.5 = (bf16[4,160,400]{2,1,0:T(8,128)(2,1)S(1)}, bf16[4,160,400]{2,1,0:T(8,128)(2,1)S(1)}, u32[]{:S(2)}, u32[]{:S(2)}) collective-permute-start(bf16[4,160,400]{2,1,0:T(8,128)(2,1)S(1)} %bitcast_dynamic-update-slice_fusion.7), channel_id=1, source_target_pairs={{0,3},{1,0},{2,1},{3,2},{4,7},{5,4},{6,5},{7,6},{8,11},{9,8},{10,9... | collective-permute-start | bytes 1536008 | tf_op jit(solution)/shard_map/ppermute | solution.py:19
  50.6 23.8 %collective-permute-start.9 = (bf16[400,3,200]{0,2,1:T(8,128)(2,1)}, bf16[400,3,200]{0,2,1:T(8,128)(2,1)S(1)}, u32[]{:S(2)}, u32[]{:S(2)}) collective-permute-start(bf16[400,3,200]{0,2,1:T(8,128)(2,1)} %pad_maximum_fusion.2), channel_id=1, source_target_pairs={{0,4},{4,8},{8,12},{12,0},{1,5},{5,9},{9,13},{13,1},{2,6},{6,10},{... | collective-permute-start | bytes 1440008 | tf_op jit(solution)/shard_map/ppermute | solution.py:19
  50.6 28.5 %collective-permute-start.10 = (bf16[400,3,200]{0,2,1:T(8,128)(2,1)}, bf16[400,3,200]{0,2,1:T(8,128)(2,1)S(1)}, u32[]{:S(2)}, u32[]{:S(2)}) collective-permute-start(bf16[400,3,200]{0,2,1:T(8,128)(2,1)} %pad_maximum_fusion.2), channel_id=1, source_target_pairs={{0,8},{4,12},{8,0},{12,4},{1,9},{5,13},{9,1},{13,5},{2,10},{6,14},... | collective-permute-start | bytes 1440008 | tf_op jit(solution)/shard_map/ppermute | solution.py:19
  61.6 23.2 %collective-permute-start.11 = (bf16[400,3,200]{0,2,1:T(8,128)(2,1)}, bf16[400,3,200]{0,2,1:T(8,128)(2,1)S(1)}, u32[]{:S(2)}, u32[]{:S(2)}) collective-permute-start(bf16[400,3,200]{0,2,1:T(8,128)(2,1)} %pad_maximum_fusion.2), channel_id=1, source_target_pairs={{0,12},{4,0},{8,4},{12,8},{1,13},{5,1},{9,5},{13,9},{2,14},{6,2},{... | collective-permute-start | bytes 1440008 | tf_op jit(solution)/shard_map/ppermute | solution.py:19
  74.4 4.8 %copy-start = (bf16[4,4,160,400]{3,2,1,0:T(8,128)(2,1)}, bf16[4,4,160,400]{3,2,1,0:T(8,128)(2,1)S(1)}, u32[]{:S(2)}) copy-start(bf16[4,4,160,400]{3,2,1,0:T(8,128)(2,1)S(1)} %bitcast_dynamic-update-slice_fusion.3) | copy-start | bytes 6144004
  196.4 3.7 %collective-permute-start.12 = (f32[320,2]{0,1:T(2,128)S(1)}, f32[320,2]{0,1:T(2,128)S(1)}, u32[]{:S(2)}, u32[]{:S(2)}) collective-permute-start(f32[320,2]{0,1:T(2,128)S(1)} %pad_maximum_fusion.3), channel_id=1, source_target_pairs={{0,1},{1,0},{2,3},{3,2},{4,5},{5,4},{6,7},{7,6},{8,9},{9,8},{10,11... | collective-permute-start | bytes 7688 | tf_op jit(solution)/shard_map/ppermute | solution.py:37
  200.1 5.2 %collective-permute-start.13 = (f32[320,2]{0,1:T(2,128)S(1)}, f32[320,2]{0,1:T(2,128)S(1)}, u32[]{:S(2)}, u32[]{:S(2)}) collective-permute-start(f32[320,2]{0,1:T(2,128)S(1)} %fusion.28), channel_id=1, source_target_pairs={{0,2},{1,3},{2,0},{3,1},{4,6},{5,7},{6,4},{7,5},{8,10},{9,11},{10,... | collective-permute-start | bytes 7688 | tf_op jit(solution)/shard_map/ppermute | solution.py:37
  207.5 8.7 %copy-start.2 = (s32[1,1280]{1,0:T(1,128)S(1)}, s32[1,1280]{1,0:T(1,128)}, u32[]{:S(2)}) copy-start(s32[1,1280]{1,0:T(1,128)} %param.12) | copy-start | bytes 15364
  207.5 28.0 %all-to-all-start = ((bf16[320,3,4,200]{0,3,1,2:T(8,128)(2,1)}), bf16[320,3,4,200]{0,3,1,2:T(8,128)(2,1)S(1)}, u32[]{:S(2)}, u32[]{:S(2)}) async-start(bf16[320,3,4,200]{0,3,1,2:T(8,128)(2,1)} %copy.65), calls=%async_computation.1 | async-start | bytes 3686400 | tf_op jit(solution)/shard_map/all_to_all | solution.py:125
  241.0 23.9 %collective-permute-start.14 = (bf16[1280,3,128]{0,2,1:T(8,128)(2,1)S(1)}, bf16[1280,3,128]{0,2,1:T(8,128)(2,1)S(1)}, u32[]{:S(2)}, u32[]{:S(2)}) collective-permute-start(bf16[1280,3,128]{0,2,1:T(8,128)(2,1)S(1)} %slice.88), channel_id=1, source_target_pairs={{4,0},{8,4},{12,8},{1,12},{5,1},{9,5},{13,9},{2,13},{6,2},{10,6},{... | collective-permute-start | bytes 2949128 | tf_op jit(solution)/shard_map/ppermute | solution.py:127
  282.6 7.1 %copy-start.3 = (s32[25]{0:T(128)S(1)}, s32[25]{0:T(128)}, u32[]{:S(2)}) copy-start(s32[25]{0:T(128)} %constant.182) | copy-start | bytes 304
  283.5 17.0 %all-to-all-start.1 = ((bf16[16,80,2,128]{3,1,2,0:T(8,128)(2,1)}), bf16[16,80,2,128]{3,1,2,0:T(8,128)(2,1)S(1)}, u32[]{:S(2)}, u32[]{:S(2)}) async-start(bf16[16,80,2,128]{3,1,2,0:T(8,128)(2,1)} %bitcast.48), calls=%async_computation.2 | async-start | bytes 1310720 | tf_op jit(solution)/shard_map/all_to_all | solution.py:153
Sparse Core Ops, SparseCore 0:
  125.5 67.1 reduce-scatter.1
